TPU v7x, 512 devices: a whole 4x4x16 slice. The times are simulated.
512 devices in a mesh: dp: 8 (over z_lo), seq: 4 (over z_hi, core), expert: 16 (over x, y).
Axes of the slice: x: 4, y: 4, z: 16 (z_hi: 2, z_lo: 8; z = z_hi * 8 + z_lo), core: 2. Of those that a mesh axis runs over, the one named last changes fastest.
Arguments:
- keys: bfloat16 [16, 4096, 512], P('expert', ('dp', 'seq')), may hold values from -4 to 4
- values: bfloat16 [16, 4096, 512], P('expert', ('dp', 'seq')), may hold values from -5 to 5
- queries: bfloat16 [16, 32, 4096], P('expert', ('dp', 'seq')), may hold values from -80 to 80
- residual: bfloat16 [16, 32, 2048], P('expert', ('dp', 'seq')), may hold values from -9 to 9
- out_proj: bfloat16 [4096, 2048], P(('dp', 'seq')), may hold values from -0.09375 to 0.09375
- norm_gain: bfloat16 [2048], replicated, may hold values from 0.25 to 1.75
- router: bfloat16 [2048, 128], replicated, may hold values from -8 to 8
- w_gate: bfloat16 [128, 2048, 768], P(('dp', 'expert'), None, 'seq'), may hold values from -0.125 to 0.125
- w_up: bfloat16 [128, 2048, 768], P(('dp', 'expert'), None, 'seq'), may hold values from -0.125 to 0.125
- w_down: bfloat16 [128, 768, 2048], P(('dp', 'expert'), 'seq'), may hold values from -0.21875 to 0.21875
- head_vec: bfloat16 [2048], replicated, may hold values from -0.09 to 0.09
- routes: int32 [16, 32, 8], P('expert', 'dp'), may hold values from 0 to 127, all different within a row; in each aligned block of 4 rows (0 to 3, 4 to 7, ..., all dimensions but the last counted through in order) at most 2 rows name the same one
- step_pos: int32 [16, 32], P('expert'), may hold values from 0 to 4095, as said below
- labels: int32 [16, 32], P('expert', ('dp', 'seq')), may hold values 0 or 1
- trace_len: int32 [16, 8], P('expert'), may hold values from 1 to 1024, 4096 in all within a row
Outputs:
- loss: float32 [], replicated
- grad_down: bfloat16 [128, 768, 2048], P(('dp', 'expert'), 'seq')
- grad_router: bfloat16 [2048, 128], P(('dp', 'seq', 'expert'))
Inputs may be any that keep to these rules, and one draw needn't show every extreme that they name: `step_pos`: increasing along each pack; distinct. `routes`: in each aligned block of 4 step ends (those of one index of dp in one pack) no expert is named by more than 2 of them.
All inputs are finite; a program needn't handle non-finite values. No bound on the sum of `labels` on one device may be relied on, other than what follows from the above.
Results may differ from a plain program's by a relative error of at most 0.018.
Values may be sent and summed in bfloat16 or wider, within the bound.
No kernel may reach another device: no remote copies, remote signals or barrier semaphores. Data moves between devices by JAX's collectives and lax.ppermute only.
A program may use at most 64 MiB of HBM per device.

v0:
```python
import jax
import jax.numpy as jnp
from jax import lax
from jax.sharding import Mesh
from jax.sharding import PartitionSpec as P

QUERY_HEADS = 32
KEY_VALUE_HEADS = 4
HEAD_WIDTH = 128
DP_EXPERT = ("dp", "expert_0", "expert_1")
DP_SEQ = ("dp", "seq_0", "seq_1")
SEQ = ("seq_0", "seq_1")
DP_SEQ_EXPERT = ("dp", "seq_0", "seq_1", "expert_0", "expert_1")
EXPERT = ("expert_0", "expert_1")
ROWS = DP_SEQ_EXPERT
MASKED = -1e30
EPSILON = 1e-06


def joined_along(blocks, dim):
    blocks = jnp.moveaxis(blocks, 0, dim)
    lengths = blocks.shape
    return blocks.reshape(*lengths[:dim], lengths[dim] * lengths[dim + 1], *lengths[dim + 2 :])


def from_everyone(array, axis):
    copies = jnp.broadcast_to(array, (lax.axis_size(axis), *array.shape))
    return lax.all_to_all(copies, axis, split_axis=0, concat_axis=0, tiled=True)


def gather_directly(array, axis, dim):
    return joined_along(from_everyone(array, axis), dim)


def in_blocks(array, dim, count):
    lengths = array.shape
    blocks = array.reshape(*lengths[:dim], count, lengths[dim] // count, *lengths[dim + 1 :])
    return jnp.moveaxis(blocks, dim, 0)


def sent_and_summed(array, axis, dim):
    count = lax.axis_size(axis)
    blocks = lax.all_to_all(in_blocks(array, dim, count), axis, 0, 0, tiled=True)
    return jnp.sum(blocks.astype(jnp.float32), axis=0)


def rms_scale(stream):
    return lax.rsqrt(jnp.mean(stream * stream, axis=-1, keepdims=True) + EPSILON)


def head_logit(final, head_vec):
    return jnp.sum(final * rms_scale(final) * head_vec.astype(jnp.float32)[None, :], axis=1)


def split_pair(value):
    high = value.astype(jnp.bfloat16)
    low = (value - high.astype(jnp.float32)).astype(jnp.bfloat16)
    return (high, low)


def join_pair(high, low):
    return high.astype(jnp.float32) + low.astype(jnp.float32)


def merge_heads(weighted_r, totals_r, peak_r):
    peak_all = jnp.max(peak_r, axis=0)
    factor = jnp.exp(peak_r - peak_all[None])
    weighted_sum = jnp.sum(weighted_r * factor[..., None], axis=0)
    totals_sum = jnp.sum(totals_r * factor, axis=0)
    merged = weighted_sum / totals_sum[..., None]
    return merged.reshape(merged.shape[0], -1).astype(jnp.bfloat16)


def shards(
    keys,
    values,
    queries,
    residual,
    out_proj,
    norm_gain,
    router,
    w_gate,
    w_up,
    w_down,
    head_vec,
    routes,
    step_pos,
    labels,
    trace_len,
):
    block_routes = lax.all_gather(routes[0], DP_EXPERT, axis=0)
    block_routes = block_routes.reshape(
        lax.axis_size("dp"), lax.axis_size(EXPERT), *routes.shape[1:]
    )
    routes_all = jnp.swapaxes(block_routes, 1, 2).reshape(-1, routes.shape[2])
    count_of_keys = keys.shape[1]
    query_groups = QUERY_HEADS // KEY_VALUE_HEADS
    query_all = gather_directly(queries, DP_SEQ, 1)[0]
    positions = step_pos[0]
    number_of_steps = positions.shape[0]
    lengths = trace_len[0]
    trace_ends = jnp.cumsum(lengths)
    starts = jnp.sum(
        jnp.where(trace_ends[None, :] <= positions[:, None], lengths[None, :], 0), axis=1
    )
    key_pos = lax.axis_index(DP_SEQ) * count_of_keys + jnp.arange(count_of_keys, dtype=jnp.int32)
    allowed = (key_pos[None, :] <= positions[:, None]) & (key_pos[None, :] >= starts[:, None])
    score_list = []
    for head_cluster in range(KEY_VALUE_HEADS):
        query_part = query_all[
            :,
            head_cluster
            * query_groups
            * HEAD_WIDTH : (head_cluster + 1)
            * query_groups
            * HEAD_WIDTH,
        ].reshape(number_of_steps * query_groups, HEAD_WIDTH)
        key_part = keys[0, :, head_cluster * HEAD_WIDTH : (head_cluster + 1) * HEAD_WIDTH]
        score_part = lax.dot_general(
            query_part, key_part, (((1,), (1,)), ((), ())), preferred_element_type=jnp.float32
        ) * HEAD_WIDTH ** (-0.5)
        score_part = score_part.reshape(number_of_steps, query_groups, count_of_keys)
        score_list.append(jnp.where(allowed[:, None, :], score_part, MASKED))
    scores = jnp.stack(score_list, axis=1).reshape(number_of_steps, QUERY_HEADS, count_of_keys)
    local_peak = jnp.max(scores, axis=2)
    heads_of_values = values[0].reshape(count_of_keys, KEY_VALUE_HEADS, HEAD_WIDTH)
    complete_weight_rows = jnp.where(
        allowed[:, None, :], jnp.exp(scores - local_peak[:, :, None]), 0.0
    )
    totals = jnp.sum(complete_weight_rows, axis=2)
    reduced_weight_rows = complete_weight_rows.astype(jnp.bfloat16).reshape(
        number_of_steps, KEY_VALUE_HEADS, query_groups, count_of_keys
    )
    weighted = jnp.einsum(
        "skgt,tkd->skgd", reduced_weight_rows, heads_of_values, preferred_element_type=jnp.float32
    ).reshape(number_of_steps, QUERY_HEADS, HEAD_WIDTH)
    totals_hi, totals_lo = split_pair(totals)
    peak_hi, peak_lo = split_pair(local_peak)
    packed = jnp.concatenate(
        [
            weighted.astype(jnp.bfloat16),
            totals_hi[..., None],
            totals_lo[..., None],
            peak_hi[..., None],
            peak_lo[..., None],
        ],
        axis=-1,
    )
    arrived = lax.all_to_all(
        packed.reshape(1, *packed.shape), DP_SEQ, split_axis=2, concat_axis=0, tiled=True
    )
    attn = merge_heads(
        arrived[..., :HEAD_WIDTH].astype(jnp.float32),
        join_pair(arrived[..., HEAD_WIDTH], arrived[..., HEAD_WIDTH + 1]),
        join_pair(arrived[..., HEAD_WIDTH + 2], arrived[..., HEAD_WIDTH + 3]),
    )
    mixed = sent_and_summed(
        jnp.dot(attn, out_proj, preferred_element_type=jnp.float32).astype(jnp.bfloat16), DP_SEQ, 0
    )
    stream = residual[0].astype(jnp.float32) + mixed
    normed = (stream * rms_scale(stream) * norm_gain.astype(jnp.float32)[None, :]).astype(
        jnp.bfloat16
    )
    normed_all = lax.all_gather(normed, ROWS, axis=0, tiled=True)
    experts = router.shape[1]
    logits = jnp.dot(normed_all, router, preferred_element_type=jnp.float32)
    chosen = (routes_all[:, :, None] == jnp.arange(experts, dtype=jnp.int32)[None, None, :]).astype(
        jnp.float32
    )
    picked = jnp.sum(chosen * logits[:, None, :], axis=2)
    gate_weight = jax.nn.softmax(picked, axis=-1)
    mine = routes_all == lax.axis_index(DP_EXPERT)
    coef = jnp.sum(jnp.where(mine, gate_weight, 0.0), axis=1)
    gate_act = jnp.dot(normed_all, w_gate[0], preferred_element_type=jnp.float32)
    up_act = jnp.dot(normed_all, w_up[0], preferred_element_type=jnp.float32)
    hidden = (jax.nn.silu(gate_act) * up_act).astype(jnp.bfloat16)
    expert_out = jnp.dot(hidden, w_down[0], preferred_element_type=jnp.float32)
    expert_mix = lax.psum_scatter(coef[:, None] * expert_out, ROWS, scatter_dimension=0, tiled=True)
    final = stream + expert_mix
    reward, pull = jax.vjp(lambda value: head_logit(value, head_vec), final)
    target = labels[0].astype(jnp.float32)
    loss_term = jax.nn.softplus(reward) - target * reward
    logit_grad = jax.nn.sigmoid(reward) - target
    (final_grad,) = pull(logit_grad)
    d_mix = final_grad.astype(jnp.bfloat16)
    d_mix_all = lax.all_gather(d_mix, ROWS, axis=0, tiled=True)
    d_mix_wide = d_mix_all.astype(jnp.float32)
    contract_rows = (((0,), (0,)), ((), ()))
    d_out = (coef[:, None] * d_mix_wide).astype(jnp.bfloat16)
    grad_down = lax.dot_general(hidden, d_out, contract_rows, preferred_element_type=jnp.float32)
    grad_down = grad_down.astype(jnp.bfloat16).reshape((1,) + grad_down.shape)
    share_dot = jnp.sum(d_mix_wide * expert_out, axis=1)
    row_count = normed_all.shape[0]
    own_row = jnp.arange(row_count, dtype=jnp.int32) == lax.axis_index(ROWS)
    payload = jnp.concatenate(
        [jnp.where(mine, share_dot[:, None], 0.0), jnp.where(own_row, loss_term, 0.0)[:, None]],
        axis=1,
    )
    summed = lax.psum(payload, ROWS)
    route_dot = summed[:, :-1]
    loss = jnp.sum(summed[:, -1])
    pick_grad = gate_weight * (route_dot - jnp.sum(gate_weight * route_dot, axis=1, keepdims=True))
    d_logits = jnp.sum(chosen * pick_grad[:, :, None], axis=1)
    router_grad_all = lax.dot_general(
        normed_all.astype(jnp.float32), d_logits, contract_rows, precision=lax.Precision.HIGHEST
    )
    own_rows = router_grad_all.shape[0] // lax.axis_size(DP_SEQ_EXPERT)
    grad_router = lax.dynamic_slice_in_dim(
        router_grad_all, lax.axis_index(DP_SEQ_EXPERT) * own_rows, own_rows, axis=0
    ).astype(jnp.bfloat16)
    return (loss, grad_down, grad_router)


def solution(mesh):
    finer = Mesh(
        mesh.devices.reshape(mesh.shape["dp"], 2, 2, 4, 4),
        ("dp", "seq_0", "seq_1", "expert_0", "expert_1"),
    )
    return jax.shard_map(
        shards,
        mesh=finer,
        in_specs=(
            P(EXPERT, DP_SEQ, None),
            P(EXPERT, DP_SEQ, None),
            P(EXPERT, DP_SEQ, None),
            P(EXPERT, DP_SEQ, None),
            P(DP_SEQ, None),
            P(),
            P(),
            P(DP_EXPERT, None, SEQ),
            P(DP_EXPERT, None, SEQ),
            P(DP_EXPERT, SEQ, None),
            P(),
            P(EXPERT, "dp", None),
            P(EXPERT, None),
            P(EXPERT, DP_SEQ),
            P(EXPERT, None),
        ),
        out_specs=(P(), P(DP_EXPERT, SEQ, None), P(DP_SEQ_EXPERT, None)),
        check_vma=False,
    )
```

profile of v0, /device:TPU:1, one launch (start us, length us, event | category | flops | bytes accessed | tf_op | source)
XLA Modules:
  0.0 3206.8 jit_solution(4722802899857417348)
XLA Ops:
  9.0 2.2 reduce.15
  12.1 16.7 all-to-all-start
  29.3 18.7 all-to-all-done
  53.0 32.4 %all_to_all.28 = bf16[1,32,32,132]{3,1,0,2:T(8,128)(2,1)S(1)} all-to-all(bf16[1,32,32,132]{3,1,0,2:T(8,128)(2,1)S(1)} %copy.165), channel_id=1, replica_groups=mesh['dp'=8,'seq_0'=2,'seq_1'=2,'expert_0'=4,'expert_1'=4] {'dp','seq_0'..., dimensions={2} | all-to-all | bytes 540672 | tf_op jit(solution)/shard_map/all_to_all | solution.py:149
  88.7 9.7 all-to-all-start.2
  98.5 15.2 all-to-all-done.2
  116.6 462.9 %all_gather.9 = s32[128,4,8]{2,1,0:T(4,128)S(1)} all-gather(s32[1,4,8]{2,1,0:T(4,128)S(1)} %copy-done.17), channel_id=1, replica_groups=mesh['dp'=8,'seq_0'=2,'seq_1'=2,'expert_0'=4,'expert_1'=4] {'dp','expert..., dimensions={0}, use_global_device_ids=true | all-gather | bytes 16512 | tf_op jit(solution)/shard_map/all_gather | solution.py:91
  580.5 593.1 %all-gather.5.cloned.1.call-done = bf16[1048576]{0:T(1024)(128)(2,1)} async-done(((bf16[2048]{0:T(1024)(128)(2,1)}), bf16[1048576]{0:T(1024)(128)(2,1)}) %all-gather.5.cloned.1.call-update) | async-done | bytes 2097168 | tf_op jit(solution)/shard_map/all_gather | solution.py:164
  1173.6 2.8 reshape.484
  1176.4 2.8 fusion.21
  1179.9 7.3 select_reduce_fusion.1
  1188.1 1.4 sub.91
  1190.7 1.4 div.48
  1192.1 1.3 copy.173
  1195.9 2.1 fusion.7
  1198.0 4.1 broadcast_multiply_fusion
  1203.5 480.3 %all-reduce.3.cloned.1.call-done = f32[512,2048]{1,0:T(8,128)} async-done(((f32[512,2048]{1,0:T(8,128)}), f32[512,2048]{1,0:T(8,128)}) %all-reduce.3.cloned.1.call-update) | async-done | bytes 4194320
  1683.8 1.5 multiply_reduce_fusion.4
  1693.2 1384.5 %all-gather.7.cloned.1.call-done = bf16[512,1,2048]{2,1,0:T(2,128)(2,1)} async-done(((bf16[1,1,2048]{2,1,0:T(2,128)(2,1)}), bf16[512,1,2048]{2,1,0:T(2,128)(2,1)}) %all-gather.7.cloned.1.call-update) | async-done | bytes 2097168 | tf_op jit(solution)/shard_map/all_gather | solution.py:186
  3077.8 4.8 fusion
  3082.6 106.9 %psum.7 = f32[512,9]{0,1:T(8,128)S(1)} all-reduce(f32[512,9]{0,1:T(8,128)S(1)} %pad_maximum_fusion.2), channel_id=1, replica_groups=mesh['dp'=8,'seq_0'=2,'seq_1'=2,'expert_0'=4,'expert_1'=4] {'dp','seq_0'..., use_global_device_ids=true, to_apply=%region_18.19 | all-reduce | flops 4608 | bytes 36864 | tf_op jit(solution)/shard_map/psum | solution.py:199
  3190.3 2.5 select_reduce_fusion
  3192.8 2.3 fusion.52
  3195.7 4.6 fusion.2
  (121 shorter events, 23.7 us)
Async XLA Ops:
  7.2 1190.9 %copy-start = (bf16[1,192,2048]{2,1,0:T(8,128)(2,1)S(1)}, bf16[1,192,2048]{2,1,0:T(8,128)(2,1)}, u32[]{:S(2)}) copy-start(bf16[1,192,2048]{2,1,0:T(8,128)(2,1)} %param.24) | copy-start | bytes 2359300
  7.2 21.7 copy-start.8
  7.2 21.8 copy-start.19
  7.2 22.0 copy-start.18
  9.0 39.7 %copy-start.7 = (bf16[1,128,512]{2,1,0:T(8,128)(2,1)S(1)}, bf16[1,128,512]{2,1,0:T(8,128)(2,1)}, u32[]{:S(2)}) copy-start(bf16[1,128,512]{2,1,0:T(8,128)(2,1)} %param.15) | copy-start | bytes 393220
  12.1 35.9 %all-to-all-start = ((bf16[32,2,2048]{2,1,0:T(2,128)(2,1)}), bf16[32,2,2048]{2,1,0:T(2,128)(2,1)S(1)}, u32[]{:S(2)}, u32[]{:S(2)}) async-start(bf16[32,2,2048]{2,1,0:T(2,128)(2,1)} %reshape.490), calls=%async_computation | async-start | bytes 524288 | tf_op jit(solution)/shard_map/all_to_all | solution.py:28
  53.0 34.1 %copy-start.1 = (bf16[128,2048]{1,0:T(8,128)(2,1)S(1)}, bf16[128,2048]{1,0:T(8,128)(2,1)}, u32[]{:S(2)}) copy-start(bf16[128,2048]{1,0:T(8,128)(2,1)} %param.19) | copy-start | bytes 1572868
  85.3 13.1 copy-start.13
  86.5 29.4 copy-start.16
  86.5 30.1 copy-start.17
  88.7 25.0 all-to-all-start.2
  98.4 1075.2 %all-gather.5.cloned.1.call-start = ((), (), s32[]{:S(2)}) async-start(), calls=%async_computation.3 | async-start | bytes 2101248 | tf_op jit(solution)/shard_map/all_gather | solution.py:164
  116.5 1567.2 %all-reduce.3.cloned.1.call-start = ((), (), s32[]{:S(2)}) async-start(), calls=%async_computation.5 | async-start | bytes 8388608
  579.9 0.6 copy-start.5
  1176.4 2.8 copy-start.2
  1198.0 4.1 copy-start.3
  1202.1 0.7 copy-start.15
  1202.1 481.7 %copy-start.10 = (f32[2048]{0:T(1024)S(1)}, f32[2048]{0:T(1024)}, u32[]{:S(2)}) copy-start(f32[2048]{0:T(1024)} %copy-done.9) | copy-start | bytes 24580
  1202.1 481.7 %copy-start.14 = (bf16[1,1,2048]{2,1,0:T(2,128)(2,1)S(1)}, bf16[1,1,2048]{2,1,0:T(2,128)(2,1)}, u32[]{:S(2)}) copy-start(bf16[1,1,2048]{2,1,0:T(2,128)(2,1)} %param.18) | copy-start | bytes 12292
  1202.2 1875.6 %all-gather.7.cloned.1.call-start = ((), (), s32[]{:S(2)}) async-start(), calls=%async_computation.4 | async-start | bytes 4202496 | tf_op jit(solution)/shard_map/all_gather | solution.py:186
  3077.8 4.8 copy-start.6
  3077.8 111.8 %copy-start.11 = (f32[512]{0:T(512)S(1)}, f32[512]{0:T(512)}, u32[]{:S(2)}) copy-start(f32[512]{0:T(512)} %reduce_max.32) | copy-start | bytes 6148
  3077.8 111.8 %copy-start.12 = (f32[512]{0:T(512)S(1)}, f32[512]{0:T(512)}, u32[]{:S(2)}) copy-start(f32[512]{0:T(512)} %fusion.45) | copy-start | bytes 6148
  3190.3 5.4 copy-start.4
  (1 other events, 0.6 us)
Sparse Core Ops, SparseCore 0:
  116.7 1056.8 all-gather.4
  1202.3 481.4 all-reduce.2
  1689.4 1388.3 all-gather.6
where the time goes:
time: 3210 us
  waiting for transfers between devices  2490 us (78%)
  blocking collectives  602 us (19%)
    all_gather x1, waiting for transfers between devices, shards(): d_mix_all = lax.all_gather(d_mix, ROWS, axis=0, tiled=True)  1380 us
    all_gather x1, waiting for transfers between devices, shards(): normed_all = lax.all_gather(normed, ROWS, axis=0, tiled=True)  593 us
    unnamed x4, waiting for transfers between devices  480 us
    all_gather x1, blocking collectives, shards(): block_routes = lax.all_gather(routes[0], DP_EXPERT, axis=0)  463 us
    psum x1, blocking collectives, shards(): summed = lax.psum(payload, ROWS)  107 us
  transfers between devices with their start and end apart: 5, of which 5 were waited for; matrix products, arithmetic and copies ran while one was open for 0% of the time, Pallas kernels for 0%

commit v1 on v0

--- a/solution.py
+++ b/solution.py
@@ -183,7 +183,9 @@
     logit_grad = jax.nn.sigmoid(reward) - target
     (final_grad,) = pull(logit_grad)
     d_mix = final_grad.astype(jnp.bfloat16)
-    d_mix_all = lax.all_gather(d_mix, ROWS, axis=0, tiled=True)
+    d_mix_all = jnp.concatenate(
+        lax.all_to_all(jnp.stack([d_mix] * lax.axis_size(ROWS)), ROWS, 0, 0), axis=0
+    )
     d_mix_wide = d_mix_all.astype(jnp.float32)
     contract_rows = (((0,), (0,)), ((), ()))
     d_out = (coef[:, None] * d_mix_wide).astype(jnp.bfloat16)

time: 3210 us -> 1970 us (0.61)
  waiting for transfers between devices: 2490 us -> 1200 us
    all_gather x1 -> x0, waiting for transfers between devices: 1380 us -> none  [shards(): d_mix_all = lax.all_gather(d_mix, ROWS, axis=0, tiled=True)]
    all_to_all x0 -> x1, waiting for transfers between devices: none -> 95.6 us  [shards(): lax.all_to_all(jnp.stack([d_mix] * lax.axis_size(ROWS)), ROWS, 0, 0)]
    unnamed x4 -> x3, waiting for transfers between devices: 480 us -> 480 us
where the time goes in v1:
time: 1970 us
  waiting for transfers between devices  1200 us (61%)
  blocking collectives  595 us (30%)
  starting transfers between devices  47.6 us (2%)
  other arithmetic  41.1 us (2%)
  local copies, waits for them, and re-layouts  40.7 us (2%)
  between operations  22 us (1%)
    all_gather x1, waiting for transfers between devices, shards(): normed_all = lax.all_gather(normed, ROWS, axis=0, tiled=True)  593 us
    unnamed x3, waiting for transfers between devices  480 us
    all_gather x1, blocking collectives, shards(): block_routes = lax.all_gather(routes[0], DP_EXPERT, axis=0)  463 us
    psum x1, blocking collectives, shards(): summed = lax.psum(payload, ROWS)  100 us
    all_to_all x1, waiting for transfers between devices, shards(): lax.all_to_all(jnp.stack([d_mix] * lax.axis_size(ROWS)), ROWS, 0, 0)  95.6 us
  transfers between devices with their start and end apart: 5, of which 5 were waited for; matrix products, arithmetic and copies ran while one was open for 0% of the time, Pallas kernels for 0%

profile of v1, /device:TPU:1, one launch (start us, length us, event | category | flops | bytes accessed | tf_op | source)
XLA Modules:
  0.0 1967.6 jit_solution(6742099308731557947)
XLA Ops:
  9.0 2.2 reduce.17
  12.1 16.7 all-to-all-start
  29.3 18.7 all-to-all-done
  52.9 32.4 %all_to_all.33 = bf16[1,32,32,132]{3,1,0,2:T(8,128)(2,1)S(1)} all-to-all(bf16[1,32,32,132]{3,1,0,2:T(8,128)(2,1)S(1)} %copy.165), channel_id=1, replica_groups=mesh['dp'=8,'seq_0'=2,'seq_1'=2,'expert_0'=4,'expert_1'=4] {'dp','seq_0'..., dimensions={2} | all-to-all | bytes 540672 | tf_op jit(solution)/shard_map/all_to_all | solution.py:149
  88.7 9.7 all-to-all-start.2
  98.5 15.2 all-to-all-done.2
  116.6 462.9 %all_gather.6 = s32[128,4,8]{2,1,0:T(4,128)S(1)} all-gather(s32[1,4,8]{2,1,0:T(4,128)S(1)} %copy-done.16), channel_id=1, replica_groups=mesh['dp'=8,'seq_0'=2,'seq_1'=2,'expert_0'=4,'expert_1'=4] {'dp','expert..., dimensions={0}, use_global_device_ids=true | all-gather | bytes 16512 | tf_op jit(solution)/shard_map/all_gather | solution.py:91
  580.4 593.1 %all-gather.3.cloned.1.call-done = bf16[1048576]{0:T(1024)(128)(2,1)} async-done(((bf16[2048]{0:T(1024)(128)(2,1)}), bf16[1048576]{0:T(1024)(128)(2,1)}) %all-gather.3.cloned.1.call-update) | async-done | bytes 2097168 | tf_op jit(solution)/shard_map/all_gather | solution.py:164
  1173.5 2.8 reshape.491
  1176.4 2.8 fusion.21
  1179.9 7.3 select_reduce_fusion.1
  1198.0 4.1 broadcast_multiply_fusion
  1203.4 480.3 %all-reduce.3.cloned.1.call-done = f32[512,2048]{1,0:T(8,128)} async-done(((f32[512,2048]{1,0:T(8,128)}), f32[512,2048]{1,0:T(8,128)}) %all-reduce.3.cloned.1.call-update) | async-done | bytes 4194320
  1688.6 4.1 stack.5
  1692.7 14.5 reduce.19
  1707.3 4.5 reshape.499
  1711.8 21.1 %all-to-all-start.3 = ((bf16[512,2,1024]{2,1,0:T(2,128)(2,1)}), bf16[512,2,1024]{2,1,0:T(2,128)(2,1)}, u32[]{:S(2)}, u32[]{:S(2)}) async-start(bf16[512,2,1024]{2,1,0:T(2,128)(2,1)} %reshape.499), calls=%async_computation.3 | async-start | bytes 4194304 | tf_op jit(solution)/shard_map/all_to_all | solution.py:187
  1736.9 95.6 %all-to-all-done.3 = bf16[512,2,1024]{2,1,0:T(2,128)(2,1)} async-done(((bf16[512,2,1024]{2,1,0:T(2,128)(2,1)}), bf16[512,2,1024]{2,1,0:T(2,128)(2,1)}, u32[]{:S(2)}, u32[]{:S(2)}) %all-to-all-start.3) | async-done | bytes 2097184 | tf_op jit(solution)/shard_map/all_to_all | solution.py:187
  1832.5 13.6 reshape.500
  1846.1 4.7 fusion.2
  1850.8 3.7 fusion
  1854.6 100.0 %psum.7 = f32[512,9]{0,1:T(8,128)S(1)} all-reduce(f32[512,9]{0,1:T(8,128)S(1)} %pad_maximum_fusion.2), channel_id=1, replica_groups=mesh['dp'=8,'seq_0'=2,'seq_1'=2,'expert_0'=4,'expert_1'=4] {'dp','seq_0'..., use_global_device_ids=true, to_apply=%region_18.19 | all-reduce | flops 4608 | bytes 36864 | tf_op jit(solution)/shard_map/psum | solution.py:201
  1955.3 2.5 select_reduce_fusion
  1957.8 2.3 fusion.52
  (122 shorter events, 30.7 us)
Async XLA Ops:
  7.2 1190.8 %copy-start = (bf16[1,192,2048]{2,1,0:T(8,128)(2,1)S(1)}, bf16[1,192,2048]{2,1,0:T(8,128)(2,1)}, u32[]{:S(2)}) copy-start(bf16[1,192,2048]{2,1,0:T(8,128)(2,1)} %param.24) | copy-start | bytes 2359300
  7.2 21.7 %copy-start.7 = (bf16[1,128,512]{2,1,0:T(8,128)(2,1)S(1)}, bf16[1,128,512]{2,1,0:T(8,128)(2,1)}, u32[]{:S(2)}) copy-start(bf16[1,128,512]{2,1,0:T(8,128)(2,1)} %param.16) | copy-start | bytes 393220
  7.2 21.8 %copy-start.18 = (s32[1,8]{1,0:T(1,128)S(1)}, s32[1,8]{1,0:T(1,128)}, u32[]{:S(2)}) copy-start(s32[1,8]{1,0:T(1,128)} %param.29) | copy-start | bytes 100
  7.2 22.0 %copy-start.17 = (s32[1,32]{1,0:T(1,128)S(1)}, s32[1,32]{1,0:T(1,128)}, u32[]{:S(2)}) copy-start(s32[1,32]{1,0:T(1,128)} %param.27) | copy-start | bytes 388
  9.0 39.7 %copy-start.6 = (bf16[1,128,512]{2,1,0:T(8,128)(2,1)S(1)}, bf16[1,128,512]{2,1,0:T(8,128)(2,1)}, u32[]{:S(2)}) copy-start(bf16[1,128,512]{2,1,0:T(8,128)(2,1)} %param.15) | copy-start | bytes 393220
  12.1 35.9 %all-to-all-start = ((bf16[32,2,2048]{2,1,0:T(2,128)(2,1)}), bf16[32,2,2048]{2,1,0:T(2,128)(2,1)S(1)}, u32[]{:S(2)}, u32[]{:S(2)}) async-start(bf16[32,2,2048]{2,1,0:T(2,128)(2,1)} %reshape.495), calls=%async_computation | async-start | bytes 524288 | tf_op jit(solution)/shard_map/all_to_all | solution.py:28
  52.9 34.1 %copy-start.2 = (bf16[128,2048]{1,0:T(8,128)(2,1)S(1)}, bf16[128,2048]{1,0:T(8,128)(2,1)}, u32[]{:S(2)}) copy-start(bf16[128,2048]{1,0:T(8,128)(2,1)} %param.19) | copy-start | bytes 1572868
  85.3 13.1 copy-start.12
  86.4 29.4 %copy-start.15 = (bf16[2048]{0:T(1024)(128)(2,1)S(1)}, bf16[2048]{0:T(1024)(128)(2,1)}, u32[]{:S(2)}) copy-start(bf16[2048]{0:T(1024)(128)(2,1)} %param.20) | copy-start | bytes 12292
  86.5 30.1 %copy-start.16 = (s32[1,4,8]{2,1,0:T(4,128)S(1)}, s32[1,4,8]{2,1,0:T(4,128)}, u32[]{:S(2)}) copy-start(s32[1,4,8]{2,1,0:T(4,128)} %param.26) | copy-start | bytes 388
  88.7 25.0 %all-to-all-start.2 = ((bf16[32,2,1024]{2,1,0:T(2,128)(2,1)}), bf16[32,2,1024]{2,1,0:T(2,128)(2,1)S(1)}, u32[]{:S(2)}, u32[]{:S(2)}) async-start(bf16[32,2,1024]{2,1,0:T(2,128)(2,1)} %reshape.497), calls=%async_computation.2 | async-start | bytes 262144 | tf_op jit(solution)/shard_map/all_to_all | solution.py:43
  98.4 1075.1 %all-gather.3.cloned.1.call-start = ((), (), s32[]{:S(2)}) async-start(), calls=%async_computation.4 | async-start | bytes 2101248 | tf_op jit(solution)/shard_map/all_gather | solution.py:164
  114.0 0.6 copy-start.8
  116.5 1567.2 %all-reduce.3.cloned.1.call-start = ((), (), s32[]{:S(2)}) async-start(), calls=%async_computation.5 | async-start | bytes 8388608
  579.8 0.6 copy-start.4
  1176.3 2.8 copy-start.3
  1202.1 0.7 copy-start.14
  1202.1 481.7 %copy-start.9 = (f32[2048]{0:T(1024)S(1)}, f32[2048]{0:T(1024)}, u32[]{:S(2)}) copy-start(f32[2048]{0:T(1024)} %copy-done.8) | copy-start | bytes 24580
  1202.1 481.7 %copy-start.13 = (bf16[1,1,2048]{2,1,0:T(2,128)(2,1)S(1)}, bf16[1,1,2048]{2,1,0:T(2,128)(2,1)}, u32[]{:S(2)}) copy-start(bf16[1,1,2048]{2,1,0:T(2,128)(2,1)} %param.18) | copy-start | bytes 12292
  1711.8 120.7 %all-to-all-start.3 = ((bf16[512,2,1024]{2,1,0:T(2,128)(2,1)}), bf16[512,2,1024]{2,1,0:T(2,128)(2,1)}, u32[]{:S(2)}, u32[]{:S(2)}) async-start(bf16[512,2,1024]{2,1,0:T(2,128)(2,1)} %reshape.499), calls=%async_computation.3 | async-start | bytes 4194304 | tf_op jit(solution)/shard_map/all_to_all | solution.py:187
  1846.1 4.7 copy-start.1
  1850.8 3.7 copy-start.5
  1850.8 103.7 %copy-start.10 = (f32[512]{0:T(512)S(1)}, f32[512]{0:T(512)}, u32[]{:S(2)}) copy-start(f32[512]{0:T(512)} %reduce_max.32) | copy-start | bytes 6148
  1850.8 103.7 %copy-start.11 = (f32[512]{0:T(512)S(1)}, f32[512]{0:T(512)}, u32[]{:S(2)}) copy-start(f32[512]{0:T(512)} %fusion.45) | copy-start | bytes 6148
Sparse Core Ops, SparseCore 0:
  116.6 1056.8 all-gather.2
  1202.2 481.4 all-reduce.2
